TPU v7x, 128 devices: a whole 4x4x4 slice. The times are simulated.
128 devices in a mesh: req: 32 (over x, z, core), tp: 4 (over y).
Axes of the slice: x: 4, y: 4, z: 4, core: 2. Of those that a mesh axis runs over, the one named last changes fastest.
Arguments:
- hidden: bfloat16 [8192, 2048], P('req', 'tp'), may hold values from -45 to 45
- routes: int32 [8192, 2], P('req'), may hold values from 0 to 7, all different within a row; in each aligned block of 256 rows (0 to 255, 256 to 511, ...) at most 128 rows name the same one
- route_weights: float32 [8192, 2], P('req'), may hold values from 0.2 to 1
- pre_gain: float32 [2048], replicated, may hold values from 0.1 to 1.9
- out_gain: float32 [2048], P('tp'), may hold values from 0.1 to 1.9
- gate_weight: bfloat16 [32, 2048, 5632], P('req', None, 'tp'), as said below
- up_weight: bfloat16 [32, 2048, 5632], P('req', None, 'tp'), as said below
- down_weight: bfloat16 [32, 5632, 2048], P('req', 'tp'), as said below
Outputs:
- residual_out: bfloat16 [8192, 2048], P('req', 'tp')
- normed_out: bfloat16 [8192, 2048], P('req', 'tp')
Inputs may be any that keep to these rules, and one draw needn't show every extreme that they name: `routes`: each row names 2 different experts; in the rows of one index of req no expert is named by more than 128 rows, a bound that some block reaches. `gate_weight`: index r holds expert r % 8. `up_weight`: index r holds expert r % 8. `down_weight`: index r holds expert r % 8.
All inputs are finite; a program needn't handle non-finite values.
Results may differ from a plain program's by a relative error of at most 0.007.
Values may be sent and summed in bfloat16 or wider, within the bound.
No kernel may reach another device: no remote copies, remote signals or barrier semaphores. Data moves between devices by JAX's collectives and lax.ppermute only.
A program may use at most 128 MiB of HBM per device.

v0:
```python
import jax
import jax.numpy as jnp
from jax import lax
from jax.sharding import PartitionSpec as P

E = 8
CAP = 128
epsilon = 1e-05


def shards(hidden, routes, route_weights, pre_gain, out_gain, gate_weight, up_weight, down_weight):
    row_count, col_part = hidden.shape
    tp_count = lax.axis_size("tp")
    req_count = lax.axis_size("req")
    full_width = col_part * tp_count
    copies = req_count // E
    slot_count = CAP // copies
    stream = hidden.astype(jnp.float32)
    whole_rows = lax.all_gather(hidden, "tp", axis=1, tiled=True).astype(jnp.float32)
    meansq = jnp.sum(whole_rows * whole_rows, axis=1) / full_width
    normed_in = (whole_rows * lax.rsqrt(meansq + epsilon)[:, None] * pre_gain[None, :]).astype(
        jnp.bfloat16
    )
    send_cols = normed_in.shape[1]
    top = routes.shape[1]
    chosen = routes.reshape(-1)
    onehot = (chosen[:, None] == jnp.arange(E, dtype=jnp.int32)[None, :]).astype(jnp.int32)
    slot_rank = jnp.sum((jnp.cumsum(onehot, axis=0) - 1) * onehot, axis=1)
    dest = slot_rank % copies * E + chosen
    out_idx = dest * slot_count + slot_rank // copies
    out_pairs = out_idx.reshape(row_count, top)
    slot_ids = jnp.arange(req_count * slot_count, dtype=jnp.int32)
    dispatch = jnp.zeros((req_count * slot_count, row_count), jnp.bool_)
    for k in range(top):
        dispatch = dispatch | (slot_ids[:, None] == out_pairs[None, :, k])
    outgoing = jnp.dot(
        dispatch.astype(jnp.bfloat16), normed_in, preferred_element_type=jnp.float32
    ).astype(jnp.bfloat16)
    outgoing = outgoing.reshape(req_count, slot_count, send_cols)
    pieces = lax.all_to_all(outgoing, "req", split_axis=0, concat_axis=0, tiled=True)
    sources, items, widths = pieces.shape
    flat_rows = pieces.reshape(sources * items, widths)
    gate_val = jnp.dot(flat_rows, gate_weight[0], preferred_element_type=jnp.float32)
    up_val = jnp.dot(flat_rows, up_weight[0], preferred_element_type=jnp.float32)
    activ = (jax.nn.silu(gate_val) * up_val).astype(jnp.bfloat16)
    partial_out = jnp.dot(activ, down_weight[0], preferred_element_type=jnp.float32)
    partial_out = lax.optimization_barrier(partial_out.astype(jnp.bfloat16)).astype(jnp.float32)
    summed = lax.psum_scatter(
        partial_out.reshape(sources, items, widths).astype(jnp.bfloat16),
        "tp",
        scatter_dimension=2,
        tiled=True,
    )
    returned = lax.all_to_all(summed, "req", split_axis=0, concat_axis=0, tiled=True)
    returned = returned.reshape(req_count * slot_count, col_part)
    picked = returned[out_idx].reshape(row_count, top, col_part).astype(jnp.float32)
    mixed = jnp.sum(picked * route_weights[:, :, None], axis=1)
    total_stream = stream + mixed
    out_sums = lax.psum(jnp.sum(total_stream * total_stream, axis=1), "tp")
    normed_out = (
        total_stream * lax.rsqrt(out_sums / full_width + epsilon)[:, None] * out_gain[None, :]
    )
    return (total_stream.astype(jnp.bfloat16), normed_out.astype(jnp.bfloat16))


def solution(mesh):
    return jax.shard_map(
        shards,
        mesh=mesh,
        in_specs=(
            P("req", "tp"),
            P("req", None),
            P("req", None),
            P(),
            P("tp"),
            P("req", None, "tp"),
            P("req", None, "tp"),
            P("req", "tp", None),
        ),
        out_specs=(P("req", "tp"), P("req", "tp")),
        check_vma=False,
    )
```

profile of v0, /device:TPU:0, one launch (start us, length us, event | category | flops | bytes accessed | tf_op | source)
XLA Modules:
  0.0 217.9 jit_solution(11316550749932052494)
XLA Ops:
  7.2 0.0 all-gather.2.cloned.1.call-start
  7.2 0.7 all-gather.2.cloned.1.call-update
  7.9 0.0 reduce-scatter.2.cloned.1.call-start
  7.9 0.8 copy.27
  8.8 0.1 eq.62
  8.9 0.1 eq.58
  9.1 1.1 reduce-window.6
  10.2 0.2 slice_reduce_fusion
  10.5 0.1 fusion.27
  10.6 0.1 reduce_sum.41
  10.7 0.1 copy.29
  10.8 0.7 fusion.31
  11.5 24.6 %all-gather.2.cloned.1.call-done = bf16[256,2048]{1,0:T(8,128)(2,1)} async-done(((bf16[256,512]{1,0:T(8,128)(2,1)}), bf16[256,2048]{1,0:T(8,128)(2,1)}) %all-gather.2.cloned.1.call-update) | async-done | bytes 1048592 | tf_op jit(solution)/shard_map/all_gather | solution.py:19
  36.1 1.7 fusion.16
  37.8 0.0 slice-start.1
  37.8 2.7 %convolution_convert_fusion = bf16[1024,2048]{1,0:T(8,128)(2,1)S(1)} fusion(bf16[256,2048]{1,0:T(8,128)(2,1)} %all-gather.2.cloned.1.call-done, f32[2048]{0:T(1024)} %param.11, f32[256]{0:T(256)S(1)} %add_rsqrt_fusion.1, s32[256]{0:T(256)S(1)} %bitcast.40, s32[256]{0:T(256)S(1)} %bitcast.39), kind=kOutput, calls=%fused_computation.8 | convolution fusion | flops 1078722560 | bytes 5254144 | tf_op jit(solution)/shard_map/dot_general | solution.py:36
  40.6 57.5 %all_to_all.10 = bf16[32,32,2048]{2,1,0:T(8,128)(2,1)S(1)} all-to-all(bf16[32,32,2048]{2,1,0:T(8,128)(2,1)S(1)} %bitcast.33), channel_id=1, replica_groups=mesh['req'=32,'tp'=4] {'req'}, dimensions={0} | all-to-all | bytes 8388608 | tf_op jit(solution)/shard_map/all_to_all | solution.py:40
  98.1 2.1 copy-done
  100.2 8.4 %fusion.4 = f32[1024,1408]{1,0:T(8,128)} fusion(bf16[1024,2048]{1,0:T(8,128)(2,1)S(1)} %bitcast.36, bf16[1,2048,1408]{2,1,0:T(8,128)(2,1)S(1)} %bitcast.43), kind=kOutput, calls=%fused_computation.5 | convolution fusion | flops 5905580032 | bytes 15728640 | tf_op jit(solution)/shard_map/dot_general | solution.py:43
  108.6 20.6 %fusion.10 = bf16[1024,2048]{1,0:T(8,128)(2,1)} fusion(bf16[1,1408,2048]{2,1,0:T(8,128)(2,1)} %param.15, f32[1024,1408]{1,0:T(8,128)} %fusion.4, bf16[1024,2048]{1,0:T(8,128)(2,1)} %bitcast.37, bf16[1,2048,1408]{2,1,0:T(8,128)(2,1)} %param.14), kind=kOutput, calls=%fused_computation.9 | convolution fusion | flops 11821907968 | bytes 25690112 | tf_op jit(solution)/shard_map/dot_general | solution.py:46
  129.3 0.0 reduce-scatter.2.cloned.1.call-update
  129.3 44.1 %reduce-scatter.2.cloned.1.call-done = bf16[32,32,512]{2,1,0:T(8,128)(2,1)} async-done(((bf16[32,32,2048]{2,1,0:T(8,128)(2,1)}), bf16[32,32,512]{2,1,0:T(8,128)(2,1)}) %reduce-scatter.2.cloned.1.call-update) | async-done | bytes 1048592 | tf_op jit(solution)/shard_map/reduce_scatter | solution.py:48
  173.4 7.4 %all-to-all-start.1 = ((bf16[32,32,512]{2,1,0:T(8,128)(2,1)}), bf16[32,32,512]{2,1,0:T(8,128)(2,1)S(1)}, u32[]{:S(2)}, u32[]{:S(2)}) async-start(bf16[32,32,512]{2,1,0:T(8,128)(2,1)} %reduce-scatter.2.cloned.1.call-done), calls=%async_computation.2 | async-start | bytes 2097152 | tf_op jit(solution)/shard_map/all_to_all | solution.py:54
  180.8 0.1 reshape.153
  181.0 0.1 copy.34
  181.2 16.3 %all-to-all-done.1 = bf16[32,32,512]{2,1,0:T(8,128)(2,1)S(1)} async-done(((bf16[32,32,512]{2,1,0:T(8,128)(2,1)}), bf16[32,32,512]{2,1,0:T(8,128)(2,1)S(1)}, u32[]{:S(2)}, u32[]{:S(2)}) %all-to-all-start.1) | async-done | bytes 1048608 | tf_op jit(solution)/shard_map/all_to_all | solution.py:54
  197.5 2.0 gather_fusion
  199.4 0.7 reshape.154
  200.1 1.3 multiply_reduce_fusion
  201.4 0.2 multiply_reduce_fusion.1
  201.6 8.6 %psum.7 = f32[256]{0:T(256)S(1)} all-reduce(f32[256]{0:T(256)S(1)} %multiply_reduce_fusion.1), channel_id=1, replica_groups=mesh['req'=32,'tp'=4] {'tp'}, use_global_device_ids=true, to_apply=%region_7.8 | all-reduce | flops 256 | bytes 2048 | tf_op jit(solution)/shard_map/psum | solution.py:59
  210.2 0.9 multiply_convert_fusion.1
  (19 shorter events, 0.1 us)
Async XLA Ops:
  7.2 29.0 %all-gather.2.cloned.1.call-start = ((), (), s32[]{:S(2)}) async-start(), calls=%async_computation.3 | async-start | bytes 1310720 | tf_op jit(solution)/shard_map/all_gather | solution.py:19
  7.9 165.5 %reduce-scatter.2.cloned.1.call-start = ((), (), s32[]{:S(2)}) async-start(), calls=%async_computation.4 | async-start | bytes 5242880 | tf_op jit(solution)/shard_map/reduce_scatter | solution.py:48
  36.1 64.1 %slice-start = ((s8[5767168]{0:T(1024)(128)(4,1)}), s8[4194304]{0:T(1024)(128)(4,1)S(1)}, s32[]{:S(2)}) async-start(s8[5767168]{0:T(1024)(128)(4,1)} %bitcast.42), calls=%async_computation.5 | async-start | bytes 8388608
  37.8 62.4 %slice-start.1 = ((s8[5767168]{0:T(1024)(128)(4,1)}), s8[1572864]{0:T(1024)(128)(4,1)S(1)}, s32[]{:S(2)}) async-start(s8[5767168]{0:T(1024)(128)(4,1)} %bitcast.42), calls=%async_computation.6 | async-start | bytes 3145728
  98.1 2.1 copy-start
  129.3 51.7 %copy-start.2 = (f32[256,2]{0,1:T(2,128)S(1)}, f32[256,2]{0,1:T(2,128)}, u32[]{:S(2)}) copy-start(f32[256,2]{0,1:T(2,128)} %param.10) | copy-start | bytes 6148
  129.3 72.1 %copy-start.1 = (bf16[256,512]{1,0:T(8,128)(2,1)S(1)}, bf16[256,512]{1,0:T(8,128)(2,1)}, u32[]{:S(2)}) copy-start(bf16[256,512]{1,0:T(8,128)(2,1)} %param.8) | copy-start | bytes 786436
  129.3 80.9 %copy-start.3 = (f32[512]{0:T(512)S(1)}, f32[512]{0:T(512)}, u32[]{:S(2)}) copy-start(f32[512]{0:T(512)} %param.12) | copy-start | bytes 6148
  173.4 24.1 %all-to-all-start.1 = ((bf16[32,32,512]{2,1,0:T(8,128)(2,1)}), bf16[32,32,512]{2,1,0:T(8,128)(2,1)S(1)}, u32[]{:S(2)}, u32[]{:S(2)}) async-start(bf16[32,32,512]{2,1,0:T(8,128)(2,1)} %reduce-scatter.2.cloned.1.call-done), calls=%async_computation.2 | async-start | bytes 2097152 | tf_op jit(solution)/shard_map/all_to_all | solution.py:54
Sparse Core Ops, SparseCore 0:
  9.7 26.4 all-gather.1
  129.4 43.9 reduce-scatter.1
where the time goes:
time: 218 us
  waiting for transfers between devices  85.7 us (39%)
  blocking collectives  66.1 us (30%)
  matrix products  31.8 us (15%)
  between operations  14.2 us (7%)
  starting transfers between devices  7.49 us (3%)
  local copies, waits for them, and re-layouts  6.53 us (3%)
  other arithmetic  6.04 us (3%)
    all_to_all x1, blocking collectives, shards(): lax.all_to_all(outgoing, 'req', split_axis=0, concat_axis=0, tiled=True)  57.5 us
    reduce_scatter x1, waiting for transfers between devices, shards(): lax.psum_scatter(partial_out.reshape(sources, items, widths).astype(jnp.b...  44.1 us
    all_gather x1, waiting for transfers between devices, shards(): lax.all_gather(hidden, 'tp', axis=1, tiled=True).astype(jnp.float32)  24.6 us
    dot_general x1, matrix products, shards(): jnp.dot(activ, down_weight[0], preferred_element_type=jnp.float32)  20.6 us
    all_to_all x1, waiting for transfers between devices, shards(): lax.all_to_all(summed, 'req', split_axis=0, concat_axis=0, tiled=True)  16.3 us
    psum x1, blocking collectives, shards(): out_sums = lax.psum(jnp.sum(total_stream * total_stream, axis=1), 'tp')  8.58 us
    dot_general x1, matrix products, shards(): jnp.dot(flat_rows, gate_weight[0], preferred_element_type=jnp.float32)  8.44 us
    all_to_all x1, starting transfers between devices, shards(): lax.all_to_all(summed, 'req', split_axis=0, concat_axis=0, tiled=True)  7.41 us
  transfers between devices with their start and end apart: 3, of which 3 were waited for; matrix products, arithmetic and copies ran while one was open for 2% of the time, Pallas kernels for 0%

commit v1 on v0

--- a/solution.py
+++ b/solution.py
@@ -8,6 +8,24 @@
 epsilon = 1e-05
 
 
+def ring_gather(array, axis, dim):
+    ways, here, step = (lax.axis_size(axis), lax.axis_index(axis), array.shape[dim])
+    lengths = [n * ways if d == dim else n for d, n in enumerate(array.shape)]
+    full = lax.dynamic_update_slice_in_dim(
+        jnp.zeros(lengths, array.dtype), array, here * step, axis=dim
+    )
+    going_up = going_down = array
+    for far in range(1, ways // 2 + 1):
+        going_up = lax.ppermute(going_up, axis, [(d, (d + 1) % ways) for d in range(ways)])
+        full = lax.dynamic_update_slice_in_dim(full, going_up, (here - far) % ways * step, axis=dim)
+        if 2 * far < ways:
+            going_down = lax.ppermute(going_down, axis, [(d, (d - 1) % ways) for d in range(ways)])
+            full = lax.dynamic_update_slice_in_dim(
+                full, going_down, (here + far) % ways * step, axis=dim
+            )
+    return full
+
+
 def shards(hidden, routes, route_weights, pre_gain, out_gain, gate_weight, up_weight, down_weight):
     row_count, col_part = hidden.shape
     tp_count = lax.axis_size("tp")
@@ -16,7 +34,7 @@
     copies = req_count // E
     slot_count = CAP // copies
     stream = hidden.astype(jnp.float32)
-    whole_rows = lax.all_gather(hidden, "tp", axis=1, tiled=True).astype(jnp.float32)
+    whole_rows = ring_gather(hidden, "tp", 1).astype(jnp.float32)
     meansq = jnp.sum(whole_rows * whole_rows, axis=1) / full_width
     normed_in = (whole_rows * lax.rsqrt(meansq + epsilon)[:, None] * pre_gain[None, :]).astype(
         jnp.bfloat16

time: 218 us -> 205 us (0.940)
  waiting for transfers between devices: 85.7 us -> 68.8 us
  starting transfers between devices: 7.49 us -> 11.1 us
    all_gather x1 -> x0, waiting for transfers between devices: 24.6 us -> none  [shards(): lax.all_gather(hidden, 'tp', axis=1, tiled=True).astype(jnp.float32)]
    ppermute x0 -> x3, waiting for transfers between devices: none -> 9.82 us  [the longest x2 9.82 us: ring_gather(): lax.ppermute(going_up, axis, [(d, (d + 1) % ways) for d in range(ways)])]
    ppermute x0 -> x3, starting transfers between devices: none -> 3.61 us  [the longest x2 2.03 us: ring_gather(): lax.ppermute(going_up, axis, [(d, (d + 1) % ways) for d in range(ways)])]
  transfers between devices with their start and end apart: 3 -> 5, of which waited for: 3 -> 4; matrix products, arithmetic and copies ran while one was open for 2% -> 2% of each run, Pallas kernels for 0% -> 0%
where the time goes in v1:
time: 205 us
  waiting for transfers between devices  68.8 us (34%)
  blocking collectives  66.9 us (33%)
  matrix products  31.4 us (15%)
  between operations  14.3 us (7%)
  starting transfers between devices  11.1 us (5%)
  local copies, waits for them, and re-layouts  7.7 us (4%)
  other arithmetic  4.67 us (2%)
    all_to_all x1, blocking collectives, shards(): lax.all_to_all(outgoing, 'req', split_axis=0, concat_axis=0, tiled=True)  58.4 us
    reduce_scatter x1, waiting for transfers between devices, shards(): lax.psum_scatter(partial_out.reshape(sources, items, widths).astype(jnp.b...  42.7 us
    dot_general x1, matrix products, shards(): jnp.dot(activ, down_weight[0], preferred_element_type=jnp.float32)  20.6 us
    all_to_all x1, waiting for transfers between devices, shards(): lax.all_to_all(summed, 'req', split_axis=0, concat_axis=0, tiled=True)  16.3 us
    ppermute x2, waiting for transfers between devices, ring_gather(): lax.ppermute(going_up, axis, [(d, (d + 1) % ways) for d in range(ways)])  9.82 us
    psum x1, blocking collectives, shards(): out_sums = lax.psum(jnp.sum(total_stream * total_stream, axis=1), 'tp')  8.56 us
    dot_general x1, matrix products, shards(): jnp.dot(flat_rows, gate_weight[0], preferred_element_type=jnp.float32)  8.45 us
    all_to_all x1, starting transfers between devices, shards(): lax.all_to_all(summed, 'req', split_axis=0, concat_axis=0, tiled=True)  7.41 us
  transfers between devices with their start and end apart: 5, of which 4 were waited for; matrix products, arithmetic and copies ran while one was open for 2% of the time, Pallas kernels for 0%

profile of v1, /device:TPU:0, one launch (start us, length us, event | category | flops | bytes accessed | tf_op | source)
XLA Modules:
  0.0 204.8 jit_solution(2388450022076485013)
XLA Ops:
  7.2 1.7 collective-permute-start
  8.9 1.6 collective-permute-start.1
  10.5 0.8 copy.27
  11.3 0.1 eq.66
  11.5 0.1 eq.62
  11.6 1.1 reduce-window.6
  12.8 0.2 slice_reduce_fusion
  13.0 0.1 fusion.27
  13.1 0.1 reduce_sum.41
  13.4 0.7 fusion.31
  14.1 2.8 %collective-permute-done = bf16[256,512]{1,0:T(8,128)(2,1)S(1)} collective-permute-done((bf16[256,512]{1,0:T(8,128)(2,1)}, bf16[256,512]{1,0:T(8,128)(2,1)S(1)}, u32[]{:S(2)}, u32[]{:S(2)}) %collective-permute-start) | collective-permute-done | bytes 262176 | tf_op jit(solution)/shard_map/ppermute | solution.py:19
  16.9 0.3 collective-permute-start.2
  17.2 0.1 broadcast_in_dim.2
  17.3 1.0 constant_dynamic-update-slice_fusion.3
  18.4 7.0 %collective-permute-done.2 = bf16[256,512]{1,0:T(8,128)(2,1)S(1)} collective-permute-done((bf16[256,512]{1,0:T(8,128)(2,1)S(1)}, bf16[256,512]{1,0:T(8,128)(2,1)S(1)}, u32[]{:S(2)}, u32[]{:S(2)}) %collective-permute-start.2) | collective-permute-done | bytes 262176 | tf_op jit(solution)/shard_map/ppermute | solution.py:19
  25.5 0.3 fusion.16
  25.8 2.3 %convolution_convert_fusion = bf16[1024,2048]{1,0:T(8,128)(2,1)S(1)} fusion(bf16[256,2048]{1,0:T(8,128)(2,1)S(1)} %constant_dynamic-update-slice_fusion, f32[2048]{0:T(1024)} %param.11, f32[256]{0:T(256)S(1)} %add_rsqrt_fusion.1, s32[256]{0:T(256)S(1)} %bitcast.40, s32[256]{0:T(256)S(1)} %bitcast.39), kind=kOutput, calls=%fused_computation.8 | convolution fusion | flops 1078722560 | bytes 5254144 | tf_op jit(solution)/shard_map/dot_general | solution.py:54
  28.1 58.4 %all_to_all.10 = bf16[32,32,2048]{2,1,0:T(8,128)(2,1)S(1)} all-to-all(bf16[32,32,2048]{2,1,0:T(8,128)(2,1)S(1)} %bitcast.33), channel_id=1, replica_groups=mesh['req'=32,'tp'=4] {'req'}, dimensions={0} | all-to-all | bytes 8388608 | tf_op jit(solution)/shard_map/all_to_all | solution.py:58
  86.5 2.1 %copy-done = bf16[32,32,2048]{2,1,0:T(8,128)(2,1)} copy-done((bf16[32,32,2048]{2,1,0:T(8,128)(2,1)}, bf16[32,32,2048]{2,1,0:T(8,128)(2,1)S(1)}, u32[]{:S(2)}) %copy-start) | copy-done | bytes 4194328
  88.5 8.5 %fusion.4 = f32[1024,1408]{1,0:T(8,128)} fusion(bf16[1024,2048]{1,0:T(8,128)(2,1)S(1)} %bitcast.36, bf16[1,2048,1408]{2,1,0:T(8,128)(2,1)S(1)} %bitcast.43), kind=kOutput, calls=%fused_computation.5 | convolution fusion | flops 5905580032 | bytes 15728640 | tf_op jit(solution)/shard_map/dot_general | solution.py:61
  97.0 20.6 %fusion.10 = bf16[1024,2048]{1,0:T(8,128)(2,1)} fusion(bf16[1,1408,2048]{2,1,0:T(8,128)(2,1)} %param.15, f32[1024,1408]{1,0:T(8,128)} %fusion.4, bf16[1024,2048]{1,0:T(8,128)(2,1)} %bitcast.37, bf16[1,2048,1408]{2,1,0:T(8,128)(2,1)} %param.14), kind=kOutput, calls=%fused_computation.9 | convolution fusion | flops 11821907968 | bytes 25690112 | tf_op jit(solution)/shard_map/dot_general | solution.py:64
  117.7 42.7 %reduce-scatter.2.cloned.1.call-done = bf16[32,32,512]{2,1,0:T(8,128)(2,1)} async-done(((bf16[32,32,2048]{2,1,0:T(8,128)(2,1)}), bf16[32,32,512]{2,1,0:T(8,128)(2,1)}) %reduce-scatter.2.cloned.1.call-update) | async-done | bytes 1048592 | tf_op jit(solution)/shard_map/reduce_scatter | solution.py:66
  160.4 7.4 %all-to-all-start.1 = ((bf16[32,32,512]{2,1,0:T(8,128)(2,1)}), bf16[32,32,512]{2,1,0:T(8,128)(2,1)S(1)}, u32[]{:S(2)}, u32[]{:S(2)}) async-start(bf16[32,32,512]{2,1,0:T(8,128)(2,1)} %reduce-scatter.2.cloned.1.call-done), calls=%async_computation.2 | async-start | bytes 2097152 | tf_op jit(solution)/shard_map/all_to_all | solution.py:72
  167.8 0.1 reshape.153
  167.9 0.1 copy.34
  168.1 16.3 %all-to-all-done.1 = bf16[32,32,512]{2,1,0:T(8,128)(2,1)S(1)} async-done(((bf16[32,32,512]{2,1,0:T(8,128)(2,1)}), bf16[32,32,512]{2,1,0:T(8,128)(2,1)S(1)}, u32[]{:S(2)}, u32[]{:S(2)}) %all-to-all-start.1) | async-done | bytes 1048608 | tf_op jit(solution)/shard_map/all_to_all | solution.py:72
  184.4 2.0 gather_fusion
  186.4 0.7 reshape.154
  187.0 1.3 multiply_reduce_fusion
  188.4 0.2 multiply_reduce_fusion.1
  188.6 8.6 %psum.7 = f32[256]{0:T(256)S(1)} all-reduce(f32[256]{0:T(256)S(1)} %multiply_reduce_fusion.1), channel_id=1, replica_groups=mesh['req'=32,'tp'=4] {'tp'}, use_global_device_ids=true, to_apply=%region_7.8 | all-reduce | flops 256 | bytes 2048 | tf_op jit(solution)/shard_map/psum | solution.py:77
  197.1 0.9 multiply_convert_fusion.1
  (27 shorter events, 0.3 us)
Async XLA Ops:
  7.2 153.2 %reduce-scatter.2.cloned.1.call-start = ((), (), s32[]{:S(2)}) async-start(), calls=%async_computation.3 | async-start | bytes 5242880 | tf_op jit(solution)/shard_map/reduce_scatter | solution.py:66
  7.2 9.7 %collective-permute-start = (bf16[256,512]{1,0:T(8,128)(2,1)}, bf16[256,512]{1,0:T(8,128)(2,1)S(1)}, u32[]{:S(2)}, u32[]{:S(2)}) collective-permute-start(bf16[256,512]{1,0:T(8,128)(2,1)} %param.8), channel_id=1, source_target_pairs={{0,1},{1,2},{2,3},{3,0},{4,5},{5,6},{6,7},{7,4},{8,9},{9,10},{10,1... | collective-permute-start | bytes 786440 | tf_op jit(solution)/shard_map/ppermute | solution.py:19
  8.9 9.5 %collective-permute-start.1 = (bf16[256,512]{1,0:T(8,128)(2,1)}, bf16[256,512]{1,0:T(8,128)(2,1)S(1)}, u32[]{:S(2)}, u32[]{:S(2)}) collective-permute-start(bf16[256,512]{1,0:T(8,128)(2,1)} %param.8), channel_id=1, source_target_pairs={{0,3},{1,0},{2,1},{3,2},{4,7},{5,4},{6,5},{7,6},{8,11},{9,8},{10,9... | collective-permute-start | bytes 786440 | tf_op jit(solution)/shard_map/ppermute | solution.py:22
  16.9 8.6 %collective-permute-start.2 = (bf16[256,512]{1,0:T(8,128)(2,1)S(1)}, bf16[256,512]{1,0:T(8,128)(2,1)S(1)}, u32[]{:S(2)}, u32[]{:S(2)}) collective-permute-start(bf16[256,512]{1,0:T(8,128)(2,1)S(1)} %collective-permute-done), channel_id=1, source_target_pairs={{0,1},{1,2},{2,3},{3,0},{4,5},{5,6},{6,7},{7,4},{8,9},{9,10},{10,1... | collective-permute-start | bytes 786440 | tf_op jit(solution)/shard_map/ppermute | solution.py:19
  25.5 63.1 %slice-start = ((s8[5767168]{0:T(1024)(128)(4,1)}), s8[4194304]{0:T(1024)(128)(4,1)S(1)}, s32[]{:S(2)}) async-start(s8[5767168]{0:T(1024)(128)(4,1)} %bitcast.42), calls=%async_computation.4 | async-start | bytes 8388608
  25.8 62.7 %slice-start.1 = ((s8[5767168]{0:T(1024)(128)(4,1)}), s8[1572864]{0:T(1024)(128)(4,1)S(1)}, s32[]{:S(2)}) async-start(s8[5767168]{0:T(1024)(128)(4,1)} %bitcast.42), calls=%async_computation.5 | async-start | bytes 3145728
  86.5 2.1 %copy-start = (bf16[32,32,2048]{2,1,0:T(8,128)(2,1)}, bf16[32,32,2048]{2,1,0:T(8,128)(2,1)S(1)}, u32[]{:S(2)}) copy-start(bf16[32,32,2048]{2,1,0:T(8,128)(2,1)S(1)} %all_to_all.10) | copy-start | bytes 12582916
  117.6 50.3 %copy-start.2 = (f32[256,2]{0,1:T(2,128)S(1)}, f32[256,2]{0,1:T(2,128)}, u32[]{:S(2)}) copy-start(f32[256,2]{0,1:T(2,128)} %param.10) | copy-start | bytes 6148
  117.7 70.7 %copy-start.1 = (bf16[256,512]{1,0:T(8,128)(2,1)S(1)}, bf16[256,512]{1,0:T(8,128)(2,1)}, u32[]{:S(2)}) copy-start(bf16[256,512]{1,0:T(8,128)(2,1)} %param.8) | copy-start | bytes 786436
  117.7 79.5 %copy-start.3 = (f32[512]{0:T(512)S(1)}, f32[512]{0:T(512)}, u32[]{:S(2)}) copy-start(f32[512]{0:T(512)} %param.12) | copy-start | bytes 6148
  160.4 24.0 %all-to-all-start.1 = ((bf16[32,32,512]{2,1,0:T(8,128)(2,1)}), bf16[32,32,512]{2,1,0:T(8,128)(2,1)S(1)}, u32[]{:S(2)}, u32[]{:S(2)}) async-start(bf16[32,32,512]{2,1,0:T(8,128)(2,1)} %reduce-scatter.2.cloned.1.call-done), calls=%async_computation.2 | async-start | bytes 2097152 | tf_op jit(solution)/shard_map/all_to_all | solution.py:72
Sparse Core Ops, SparseCore 0:
  117.8 42.5 reduce-scatter.1
